TPU v7x, 512 devices: a whole 4x8x8 slice. The times are simulated.
512 devices in a mesh: seq: 64 (over z, y), chan: 8 (over x, core).
Axes of the slice: x: 4, y: 8, z: 8, core: 2. Of those that a mesh axis runs over, the one named last changes fastest.
Arguments:
- tokens: bfloat16 [8192, 4096], P('seq', 'chan'), may hold values from -6 to 6
- conv_taps: float32 [4, 4096], P(None, 'chan'), may hold values from -12 to 12
- log_rate: float32 [4096], P('chan'), may hold values from 4.8828125e-06 to 0.034
- rotation: float32 [4096], P('chan'), may hold values from 0 to 0.2
- in_proj: bfloat16 [64, 64, 128], P('chan'), may hold values from -0.75 to 0.75
- out_proj: bfloat16 [64, 64, 128], P('chan'), may hold values from -0.5 to 0.5
- skip_gain: float32 [4096], P('chan'), may hold values from 0.25 to 1.5
- norm_gain: float32 [4096], P('chan'), may hold values from 0.25 to 1.75
- retention: float32 [8192], P('seq'), may hold values from 0.5 to 1
- cotangent: bfloat16 [8192, 4096], P('seq', 'chan'), may hold values from -6 to 6
Outputs:
- normed: bfloat16 [8192, 4096], P('seq', 'chan')
- tokens_grad: bfloat16 [8192, 4096], P('seq', 'chan')
- in_grad: float32 [64, 64, 128], P('chan')
- out_grad: float32 [64, 64, 128], P('chan')
- taps_grad: float32 [4, 4096], P(None, 'chan')
All inputs are finite; a program needn't handle non-finite values.
Results may differ from a plain program's by a relative error of at most 0.011.
Values may be sent and summed in bfloat16 or wider, within the bound.
No kernel may reach another device: no remote copies, remote signals or barrier semaphores. Data moves between devices by JAX's collectives and lax.ppermute only.
A program may use at most 64 MiB of HBM per device.

v0:
```python
import jax
import jax.numpy as jnp
from jax import lax
from jax.sharding import Mesh, PartitionSpec as P

SEQ = ("z", "y")


def from_behind(value, axis, by):
    length = lax.axis_size(axis)
    pairs = [(i, i + by) for i in range(length) if 0 <= i + by < length]
    return lax.ppermute(value, axis, pairs)


def carried_in(part, axis, combine, identity, reverse):
    count = lax.axis_size(axis)
    place = lax.axis_index(axis)
    ahead = count - 1 - place if reverse else place
    step = -1 if reverse else 1
    packed = jnp.stack(part)
    unit = jnp.stack([jnp.zeros_like(a) + jnp.asarray(e, a.dtype) for a, e in zip(part, identity)])
    state = jnp.where(ahead >= 1, from_behind(packed, axis, step), unit)
    reach = 1
    while reach < count:
        earlier = from_behind(state, axis, step * reach)
        joined = jnp.stack(combine(tuple(earlier), tuple(state)))
        state = jnp.where(ahead >= reach, joined, state)
        reach *= 2
    return tuple(state)


def linear_run(drive_re, drive_im, decay_rate, turn_rate, log_keep):
    seq_len, num_cols = drive_re.shape
    block_len = min(64, seq_len)
    block_count = seq_len // block_len
    offsets = jnp.arange(block_len, dtype=jnp.float32)
    keep_cum = jnp.cumsum(log_keep.reshape(block_count, block_len), axis=1)[:, :, None]
    angles = offsets[:, None] * turn_rate[None, :]
    cosine = jnp.cos(angles)
    sine = jnp.sin(angles)
    growth = jnp.exp(offsets[None, :, None] * decay_rate[None, None, :] - keep_cum)
    blk_re = drive_re.reshape(block_count, block_len, num_cols)
    blk_im = drive_im.reshape(block_count, block_len, num_cols)
    pre_re = growth * (blk_re * cosine + blk_im * sine)
    pre_im = growth * (blk_im * cosine - blk_re * sine)
    lower_ones = (offsets[:, None] >= offsets[None, :]).astype(jnp.float32)
    summed = jnp.einsum(
        "ji,abik->abjk", lower_ones, jnp.stack([pre_re, pre_im]), precision=lax.Precision.HIGHEST
    )
    shrink = jnp.exp(keep_cum - offsets[None, :, None] * decay_rate[None, None, :])
    state_re = shrink * (summed[0] * cosine - summed[1] * sine)
    state_im = shrink * (summed[0] * sine + summed[1] * cosine)
    step_mag = jnp.exp(keep_cum[:, -1] - block_len * decay_rate[None, :])
    step_re = step_mag * jnp.cos(block_len * turn_rate)[None, :]
    step_im = step_mag * jnp.sin(block_len * turn_rate)[None, :]

    def advance(carried, inputs):
        carry_re, carry_im = carried
        mult_re, mult_im, end_re, end_im = inputs
        next_re = mult_re * carry_re - mult_im * carry_im + end_re
        next_im = mult_re * carry_im + mult_im * carry_re + end_im
        return ((next_re, next_im), (carry_re, carry_im))

    zeros_col = jnp.zeros((num_cols,), jnp.float32)
    enter_re, enter_im = lax.scan(
        advance, (zeros_col, zeros_col), (step_re, step_im, state_re[:, -1], state_im[:, -1])
    )[1]
    ahead = offsets + 1.0
    lift = jnp.exp(keep_cum - ahead[None, :, None] * decay_rate[None, None, :])
    lift_re = lift * jnp.cos(ahead[:, None] * turn_rate[None, :])
    lift_im = lift * jnp.sin(ahead[:, None] * turn_rate[None, :])
    state_re = state_re + lift_re * enter_re[:, None] - lift_im * enter_im[:, None]
    state_im = state_im + lift_re * enter_im[:, None] + lift_im * enter_re[:, None]
    return (state_re.reshape(seq_len, num_cols), state_im.reshape(seq_len, num_cols))


def carry_combine(earlier, later):
    early_re, early_im, early_sre, early_sim = earlier
    late_re, late_im, late_sre, late_sim = later
    joined_re = early_re * late_re - early_im * late_im
    joined_im = early_re * late_im + early_im * late_re
    joined_sre = late_re * early_sre - late_im * early_sim + late_sre
    joined_sim = late_re * early_sim + late_im * early_sre + late_sim
    return (joined_re, joined_im, joined_sre, joined_sim)


def per_device(
    tokens,
    conv_taps,
    log_rate,
    rotation,
    in_proj,
    out_proj,
    skip_gain,
    norm_gain,
    retention,
    cotangent,
):
    seq_len, local_width = tokens.shape
    tap_count = conv_taps.shape[0]
    local_heads, head_width, double_state = in_proj.shape
    state_size = double_state // 2
    num_cols = local_heads * state_size
    lead_rows = from_behind(tokens[seq_len - (tap_count - 1) :], SEQ, 1)
    padded = jnp.concatenate([lead_rows, tokens], axis=0).astype(jnp.float32)
    conv_sum = conv_taps[0][None, :] * padded[tap_count - 1 :]
    for offset in range(1, tap_count):
        conv_sum = (
            conv_sum
            + conv_taps[offset][None, :]
            * padded[tap_count - 1 - offset : tap_count - 1 - offset + seq_len]
        )
    mixed_in = conv_sum.astype(jnp.bfloat16)
    by_head = mixed_in.reshape(seq_len, local_heads, head_width)
    projected = jnp.einsum("thc,hck->thk", by_head, in_proj, preferred_element_type=jnp.float32)
    in_scale = jnp.sqrt(-jnp.expm1(-2.0 * log_rate))
    drive_re = projected[:, :, :state_size].reshape(seq_len, num_cols) * in_scale
    drive_im = projected[:, :, state_size:].reshape(seq_len, num_cols) * in_scale
    log_keep = jnp.log(retention)
    state_re, state_im = linear_run(drive_re, drive_im, log_rate, rotation, log_keep)
    keep_total = jnp.sum(log_keep)
    total_mag = jnp.exp(keep_total - seq_len * log_rate)
    total_re = total_mag * jnp.cos(seq_len * rotation)
    total_im = total_mag * jnp.sin(seq_len * rotation)
    unit_ones = jnp.ones((num_cols,), jnp.float32)
    zeros_col = jnp.zeros((num_cols,), jnp.float32)
    chained = carried_in(
        (total_re, total_im, state_re[-1], state_im[-1]),
        SEQ,
        carry_combine,
        (unit_ones, zeros_col, zeros_col, zeros_col),
        False,
    )
    enter_re, enter_im = (chained[2], chained[3])
    positions = jnp.arange(seq_len, dtype=jnp.float32)
    ahead = positions + 1.0
    lift = jnp.exp(jnp.cumsum(log_keep)[:, None] - ahead[:, None] * log_rate[None, :])
    lift_re = lift * jnp.cos(ahead[:, None] * rotation[None, :])
    lift_im = lift * jnp.sin(ahead[:, None] * rotation[None, :])
    state_re = state_re + lift_re * enter_re[None, :] - lift_im * enter_im[None, :]
    state_im = state_im + lift_re * enter_im[None, :] + lift_im * enter_re[None, :]
    state_bf = jnp.concatenate(
        [
            state_re.reshape(seq_len, local_heads, state_size),
            state_im.reshape(seq_len, local_heads, state_size),
        ],
        axis=2,
    ).astype(jnp.bfloat16)
    mixed = jnp.einsum(
        "thk,hck->thc", state_bf, out_proj, preferred_element_type=jnp.float32
    ).reshape(seq_len, local_width)
    mixed = mixed + skip_gain * mixed_in.astype(jnp.float32)
    squares = jnp.sum(mixed * mixed, axis=1)
    scaled = cotangent.astype(jnp.float32) * norm_gain
    dots = jnp.sum(scaled * mixed, axis=1)
    squares = lax.psum(squares, "chan")
    model_width = local_width * lax.axis_size("chan")
    inverse = lax.rsqrt(squares / model_width + 1e-06)
    normed = (mixed * inverse[:, None] * norm_gain).astype(jnp.bfloat16)
    dots = lax.psum(dots, "chan")
    mixed_grad = inverse[:, None] * (
        scaled - mixed * (inverse * inverse * dots / model_width)[:, None]
    )
    grad_bf = mixed_grad.astype(jnp.bfloat16).reshape(seq_len, local_heads, head_width)
    state_grad = jnp.einsum("thc,hck->thk", grad_bf, out_proj, preferred_element_type=jnp.float32)
    out_grad = jnp.einsum("thc,thk->hck", grad_bf, state_bf, preferred_element_type=jnp.float32)
    out_grad = lax.psum(lax.psum(out_grad, "y"), "z")
    back_keep = jnp.concatenate([jnp.zeros((1,), jnp.float32), log_keep[::-1][:-1]])
    grad_re = state_grad[:, :, :state_size].reshape(seq_len, num_cols)[::-1]
    grad_im = state_grad[:, :, state_size:].reshape(seq_len, num_cols)[::-1]
    adj_re, adj_im = linear_run(grad_re, grad_im, log_rate, -rotation, back_keep)
    first_mag = jnp.exp(log_keep[0] - log_rate)
    cos_turn = jnp.cos(rotation)
    sin_turn = jnp.sin(rotation)
    first_re = first_mag * (cos_turn * adj_re[-1] + sin_turn * adj_im[-1])
    first_im = first_mag * (cos_turn * adj_im[-1] - sin_turn * adj_re[-1])
    back_chained = carried_in(
        (total_re, -total_im, first_re, first_im),
        SEQ,
        carry_combine,
        (unit_ones, zeros_col, zeros_col, zeros_col),
        True,
    )
    later_re, later_im = (back_chained[2], back_chained[3])
    back_lift = jnp.exp(jnp.cumsum(back_keep)[:, None] - positions[:, None] * log_rate[None, :])
    back_re = back_lift * jnp.cos(positions[:, None] * rotation[None, :])
    back_im = -back_lift * jnp.sin(positions[:, None] * rotation[None, :])
    adj_re = adj_re + back_re * later_re[None, :] - back_im * later_im[None, :]
    adj_im = adj_im + back_re * later_im[None, :] + back_im * later_re[None, :]
    adj_re = adj_re[::-1]
    adj_im = adj_im[::-1]
    drive_grad = jnp.concatenate(
        [
            (in_scale * adj_re).reshape(seq_len, local_heads, state_size),
            (in_scale * adj_im).reshape(seq_len, local_heads, state_size),
        ],
        axis=2,
    ).astype(jnp.bfloat16)
    in_grad = jnp.einsum("thc,thk->hck", by_head, drive_grad, preferred_element_type=jnp.float32)
    input_grad = jnp.einsum(
        "thk,hck->thc", drive_grad, in_proj, preferred_element_type=jnp.float32
    ).reshape(seq_len, local_width)
    input_grad = input_grad + skip_gain * mixed_grad
    trail_rows = from_behind(input_grad[: tap_count - 1], SEQ, -1)
    tail = jnp.concatenate([input_grad, trail_rows], axis=0)
    tokens_grad = conv_taps[0][None, :] * tail[:seq_len]
    for offset in range(1, tap_count):
        tokens_grad = tokens_grad + conv_taps[offset][None, :] * tail[offset : offset + seq_len]
    taps_grad = jnp.stack(
        [
            jnp.sum(
                input_grad * padded[tap_count - 1 - offset : tap_count - 1 - offset + seq_len],
                axis=0,
            )
            for offset in range(tap_count)
        ]
    )
    packed = jnp.concatenate([in_grad.reshape(-1), taps_grad.reshape(-1)])
    packed = lax.psum(lax.psum(packed, "y"), "z")
    in_grad = packed[: in_grad.size].reshape(in_grad.shape)
    taps_grad = packed[in_grad.size :].reshape(taps_grad.shape)
    return (normed, tokens_grad.astype(jnp.bfloat16), in_grad, out_grad, taps_grad)


def solution(mesh):
    seq_count, chan_count = mesh.devices.shape
    inner = 1
    while inner * inner < seq_count:
        inner *= 2
    devices = mesh.devices.reshape(seq_count // inner, inner, chan_count)
    mesh = Mesh(devices, SEQ + ("chan",))
    in_specs = (
        P(SEQ, "chan"),
        P(None, "chan"),
        P("chan"),
        P("chan"),
        P("chan", None, None),
        P("chan", None, None),
        P("chan"),
        P("chan"),
        P(SEQ),
        P(SEQ, "chan"),
    )
    out_specs = (
        P(SEQ, "chan"),
        P(SEQ, "chan"),
        P("chan", None, None),
        P("chan", None, None),
        P(None, "chan"),
    )
    return jax.shard_map(
        per_device, mesh=mesh, in_specs=in_specs, out_specs=out_specs, check_vma=False
    )
```

profile of v0, /device:TPU:2, one launch (start us, length us, event | category | flops | bytes accessed | tf_op | source)
XLA Modules:
  0.0 364.7 jit_solution(13326804845153230500)
XLA Ops:
  8.2 3.5 collective-permute-start
  14.9 1.3 fusion.68
  16.2 2.5 multiply_cosine_fusion.1
  21.0 1.0 fusion.18
  27.2 3.5 collective-permute-start.1
  30.7 1.3 collective-permute-done.1
  32.1 4.2 %collective-permute-start.2 = (f32[4,512]{1,0:T(4,128)S(1)}, f32[4,512]{1,0:T(4,128)S(1)}, u32[]{:S(2)}, u32[]{:S(2)}) collective-permute-start(f32[4,512]{1,0:T(4,128)S(1)} %broadcast_select_fusion.5), channel_id=1, source_target_pairs={{0,8},{8,16},{16,24},{24,32},{32,40},{40,48},{48,56},{56,64},{64,7... | collective-permute-start | bytes 24584 | tf_op jit(solution)/shard_map/ppermute | solution.py:12
  36.2 1.3 collective-permute-done.2
  37.6 5.7 %collective-permute-start.3 = (f32[4,512]{1,0:T(4,128)S(1)}, f32[4,512]{1,0:T(4,128)S(1)}, u32[]{:S(2)}, u32[]{:S(2)}) collective-permute-start(f32[4,512]{1,0:T(4,128)S(1)} %maximum_select_fusion), channel_id=1, source_target_pairs={{0,16},{8,24},{16,32},{24,40},{32,48},{40,56},{48,64},{56,72},{64,... | collective-permute-start | bytes 24584 | tf_op jit(solution)/shard_map/ppermute | solution.py:12
  43.4 1.3 collective-permute-done.3
  44.8 10.6 %collective-permute-start.4 = (f32[4,512]{1,0:T(4,128)S(1)}, f32[4,512]{1,0:T(4,128)S(1)}, u32[]{:S(2)}, u32[]{:S(2)}) collective-permute-start(f32[4,512]{1,0:T(4,128)S(1)} %maximum_select_fusion.1), channel_id=1, source_target_pairs={{0,32},{8,40},{16,48},{24,56},{32,64},{40,72},{48,80},{56,88},{64,... | collective-permute-start | bytes 24584 | tf_op jit(solution)/shard_map/ppermute | solution.py:12
  55.4 1.3 collective-permute-done.4
  56.8 9.1 %collective-permute-start.5 = (f32[4,512]{1,0:T(4,128)S(1)}, f32[4,512]{1,0:T(4,128)S(1)}, u32[]{:S(2)}, u32[]{:S(2)}) collective-permute-start(f32[4,512]{1,0:T(4,128)S(1)} %maximum_select_fusion.2), channel_id=1, source_target_pairs={{0,64},{8,72},{16,80},{24,88},{32,96},{40,104},{48,112},{56,120},{... | collective-permute-start | bytes 24584 | tf_op jit(solution)/shard_map/ppermute | solution.py:12
  65.9 1.3 collective-permute-done.5
  67.4 6.1 %collective-permute-start.6 = (f32[4,512]{1,0:T(4,128)S(1)}, f32[4,512]{1,0:T(4,128)S(1)}, u32[]{:S(2)}, u32[]{:S(2)}) collective-permute-start(f32[4,512]{1,0:T(4,128)S(1)} %maximum_select_fusion.3), channel_id=1, source_target_pairs={{0,128},{8,136},{16,144},{24,152},{32,160},{40,168},{48,176},{56,1... | collective-permute-start | bytes 24584 | tf_op jit(solution)/shard_map/ppermute | solution.py:12
  73.5 1.3 collective-permute-done.6
  76.1 17.7 %collective-permute-start.7 = (f32[4,512]{1,0:T(4,128)}, f32[4,512]{1,0:T(4,128)}, u32[]{:S(2)}, u32[]{:S(2)}) collective-permute-start(f32[4,512]{1,0:T(4,128)} %maximum_select_fusion.4), channel_id=1, source_target_pairs={{0,256},{8,264},{16,272},{24,280},{32,288},{40,296},{48,304},{56,3... | collective-permute-start | bytes 24584 | tf_op jit(solution)/shard_map/ppermute | solution.py:12
  97.4 1.1 sub.357
  99.4 0.9 copy.136
  100.3 0.9 copy.138
  102.5 0.9 copy.140
  108.8 1.1 squeeze.79
  109.9 0.9 copy.141
  111.7 0.9 copy.135
  113.0 0.9 multiply_subtract_fusion.7
  115.5 2.7 subtract_convert_fusion
  119.7 10.2 %all-reduce = (f32[128]{0:T(128)S(1)}, f32[128]{0:T(128)S(1)}) all-reduce(f32[128]{0:T(128)S(1)} %get-tuple-element.185, f32[128]{0:T(128)S(1)} %get-tuple-element.184), channel_id=1, replica_groups=mesh['z'=8,'y'=8,'chan'=8] {'chan'}, use_global_device_ids=true, to_apply=%region_6.7 | all-reduce | flops 256 | bytes 2048 | tf_op jit(solution)/shard_map/psum | solution.py:156
  137.2 1.3 collective-permute-start.8
  138.5 4.2 %collective-permute-done.8 = f32[4,512]{1,0:T(4,128)S(1)} collective-permute-done((f32[4,512]{1,0:T(4,128)S(1)}, f32[4,512]{1,0:T(4,128)S(1)}, u32[]{:S(2)}, u32[]{:S(2)}) %collective-permute-start.8) | collective-permute-done | bytes 8224 | tf_op jit(solution)/shard_map/ppermute | solution.py:12
  142.7 1.3 collective-permute-start.9
  144.0 4.2 %collective-permute-done.9 = f32[4,512]{1,0:T(4,128)S(1)} collective-permute-done((f32[4,512]{1,0:T(4,128)S(1)}, f32[4,512]{1,0:T(4,128)S(1)}, u32[]{:S(2)}, u32[]{:S(2)}) %collective-permute-start.9) | collective-permute-done | bytes 8224 | tf_op jit(solution)/shard_map/ppermute | solution.py:12
  148.3 1.3 collective-permute-start.10
  149.6 5.1 %collective-permute-done.10 = f32[4,512]{1,0:T(4,128)S(1)} collective-permute-done((f32[4,512]{1,0:T(4,128)S(1)}, f32[4,512]{1,0:T(4,128)S(1)}, u32[]{:S(2)}, u32[]{:S(2)}) %collective-permute-start.10) | collective-permute-done | bytes 8224 | tf_op jit(solution)/shard_map/ppermute | solution.py:12
  154.8 1.3 collective-permute-start.11
  156.1 8.1 %collective-permute-done.11 = f32[4,512]{1,0:T(4,128)S(1)} collective-permute-done((f32[4,512]{1,0:T(4,128)S(1)}, f32[4,512]{1,0:T(4,128)S(1)}, u32[]{:S(2)}, u32[]{:S(2)}) %collective-permute-start.11) | collective-permute-done | bytes 8224 | tf_op jit(solution)/shard_map/ppermute | solution.py:12
  164.3 1.3 collective-permute-start.12
  165.6 4.3 %collective-permute-done.12 = f32[4,512]{1,0:T(4,128)S(1)} collective-permute-done((f32[4,512]{1,0:T(4,128)S(1)}, f32[4,512]{1,0:T(4,128)S(1)}, u32[]{:S(2)}, u32[]{:S(2)}) %collective-permute-start.12) | collective-permute-done | bytes 8224 | tf_op jit(solution)/shard_map/ppermute | solution.py:12
  170.0 1.3 collective-permute-start.13
  172.3 4.1 %collective-permute-done.13 = f32[4,512]{1,0:T(4,128)S(1)} collective-permute-done((f32[4,512]{1,0:T(4,128)S(1)}, f32[4,512]{1,0:T(4,128)S(1)}, u32[]{:S(2)}, u32[]{:S(2)}) %collective-permute-start.13) | collective-permute-done | bytes 8224 | tf_op jit(solution)/shard_map/ppermute | solution.py:12
  176.5 1.3 collective-permute-start.14
  177.8 1.0 fusion.35
  178.8 7.2 %collective-permute-done.14 = f32[4,512]{1,0:T(4,128)S(1)} collective-permute-done((f32[4,512]{1,0:T(4,128)S(1)}, f32[4,512]{1,0:T(4,128)S(1)}, u32[]{:S(2)}, u32[]{:S(2)}) %collective-permute-start.14) | collective-permute-done | bytes 8224 | tf_op jit(solution)/shard_map/ppermute | solution.py:12
  186.7 1.1 multiply_subtract_fusion
  192.1 80.6 %all-reduce.6.cloned.1.call-done = (f32[67584]{0:T(1024)}, f32[8,64,128]{2,1,0:T(8,128)}) async-done(((f32[67584]{0:T(1024)}, f32[8,64,128]{2,1,0:T(8,128)}), (f32[67584]{0:T(1024)}, f32[8,64,128]{2,1,0:T(8,128)})) %all-reduce.6.cloned.1.call-update) | async-done | bytes 532496 | tf_op jit(solution)/shard_map/psum | solution.py:219
  272.7 1.3 collective-permute-start.15
  274.8 6.2 %collective-permute-done.15 = f32[3,512]{0,1:T(8,128)S(1)} collective-permute-done((f32[3,512]{0,1:T(8,128)S(1)}, f32[3,512]{0,1:T(8,128)S(1)}, u32[]{:S(2)}, u32[]{:S(2)}) %collective-permute-start.15) | collective-permute-done | bytes 6176 | tf_op jit(solution)/shard_map/ppermute | solution.py:12
  282.5 71.6 %all-reduce.8.cloned.1.call-done = (f32[67584]{0:T(1024)}, f32[8,64,128]{2,1,0:T(8,128)}) async-done(((f32[67584]{0:T(1024)}, f32[8,64,128]{2,1,0:T(8,128)}), (f32[67584]{0:T(1024)}, f32[8,64,128]{2,1,0:T(8,128)})) %all-reduce.8.cloned.1.call-update) | async-done | bytes 532496 | tf_op jit(solution)/shard_map/psum | solution.py:219
  354.1 1.7 slice.228
  (359 shorter events, 45.8 us)
Async XLA Ops:
  7.2 111.1 %copy-start = (bf16[8,64,128]{2,1,0:T(8,128)(2,1)S(1)}, bf16[8,64,128]{2,1,0:T(8,128)(2,1)}, u32[]{:S(2)}) copy-start(bf16[8,64,128]{2,1,0:T(8,128)(2,1)} %param.19) | copy-start | bytes 393220
  7.2 265.5 %all-reduce.6.cloned.1.call-start = ((), (), s32[]{:S(2)}) async-start(), calls=%async_computation | async-start | bytes 1064960 | tf_op jit(solution)/shard_map/psum | solution.py:219
  8.1 3.5 copy-start.88
  8.2 13.9 %collective-permute-start = (bf16[3,512]{0,1:T(8,128)(2,1)S(1)}, bf16[3,512]{0,1:T(8,128)(2,1)S(1)}, u32[]{:S(2)}, u32[]{:S(2)}) collective-permute-start(bf16[3,512]{0,1:T(8,128)(2,1)S(1)} %copy.131), channel_id=1, source_target_pairs={{0,8},{8,16},{16,24},{24,32},{32,40},{40,48},{48,56},{56,64},{64,7... | collective-permute-start | bytes 9224 | tf_op jit(solution)/shard_map/ppermute | solution.py:12
  14.2 81.8 %copy-start.72 = (f32[2,64]{1,0:T(2,128)}, f32[2,64]{1,0:T(2,128)S(1)}, u32[]{:S(2)}) copy-start(f32[2,64]{1,0:T(2,128)S(1)} %reduce.6) | copy-start | bytes 1540
  16.2 8.3 %copy-start.57 = (f32[512]{0:T(512)}, f32[512]{0:T(512)S(1)}, u32[]{:S(2)}) copy-start(f32[512]{0:T(512)S(1)} %get-tuple-element.356) | copy-start | bytes 6148
  16.2 11.0 %copy-start.59 = (f32[512]{0:T(512)}, f32[512]{0:T(512)S(1)}, u32[]{:S(2)}) copy-start(f32[512]{0:T(512)S(1)} %get-tuple-element.352) | copy-start | bytes 6148
  18.7 1.5 copy-start.14
  20.2 2.0 copy-start.49
  20.3 2.0 copy-start.51
  20.3 2.0 copy-start.53
  20.3 2.0 copy-start.55
  27.2 4.8 %collective-permute-start.1 = (f32[4,512]{1,0:T(4,128)S(1)}, f32[4,512]{1,0:T(4,128)S(1)}, u32[]{:S(2)}, u32[]{:S(2)}) collective-permute-start(f32[4,512]{1,0:T(4,128)S(1)} %fusion.48), channel_id=1, source_target_pairs={{0,8},{8,16},{16,24},{24,32},{32,40},{40,48},{48,56},{56,64},{64,7... | collective-permute-start | bytes 24584 | tf_op jit(solution)/shard_map/ppermute | solution.py:12
  32.1 5.5 %collective-permute-start.2 = (f32[4,512]{1,0:T(4,128)S(1)}, f32[4,512]{1,0:T(4,128)S(1)}, u32[]{:S(2)}, u32[]{:S(2)}) collective-permute-start(f32[4,512]{1,0:T(4,128)S(1)} %broadcast_select_fusion.5), channel_id=1, source_target_pairs={{0,8},{8,16},{16,24},{24,32},{32,40},{40,48},{48,56},{56,64},{64,7... | collective-permute-start | bytes 24584 | tf_op jit(solution)/shard_map/ppermute | solution.py:12
  37.6 7.1 %collective-permute-start.3 = (f32[4,512]{1,0:T(4,128)S(1)}, f32[4,512]{1,0:T(4,128)S(1)}, u32[]{:S(2)}, u32[]{:S(2)}) collective-permute-start(f32[4,512]{1,0:T(4,128)S(1)} %maximum_select_fusion), channel_id=1, source_target_pairs={{0,16},{8,24},{16,32},{24,40},{32,48},{40,56},{48,64},{56,72},{64,... | collective-permute-start | bytes 24584 | tf_op jit(solution)/shard_map/ppermute | solution.py:12
  44.7 30.2 %copy-start.17 = (f32[1,512]{1,0:T(1,128)}, f32[1,512]{1,0:T(1,128)S(1)}, u32[]{:S(2)}) copy-start(f32[1,512]{1,0:T(1,128)S(1)} %get-tuple-element.319) | copy-start | bytes 6148
  44.7 30.2 %copy-start.19 = (f32[1,512]{1,0:T(1,128)}, f32[1,512]{1,0:T(1,128)S(1)}, u32[]{:S(2)}) copy-start(f32[1,512]{1,0:T(1,128)S(1)} %get-tuple-element.320) | copy-start | bytes 6148
  44.7 30.2 %copy-start.21 = (f32[1,512]{1,0:T(1,128)}, f32[1,512]{1,0:T(1,128)S(1)}, u32[]{:S(2)}) copy-start(f32[1,512]{1,0:T(1,128)S(1)} %get-tuple-element.321) | copy-start | bytes 6148
  44.8 30.2 %copy-start.23 = (f32[1,512]{1,0:T(1,128)}, f32[1,512]{1,0:T(1,128)S(1)}, u32[]{:S(2)}) copy-start(f32[1,512]{1,0:T(1,128)S(1)} %get-tuple-element.322) | copy-start | bytes 6148
  44.8 11.9 %collective-permute-start.4 = (f32[4,512]{1,0:T(4,128)S(1)}, f32[4,512]{1,0:T(4,128)S(1)}, u32[]{:S(2)}, u32[]{:S(2)}) collective-permute-start(f32[4,512]{1,0:T(4,128)S(1)} %maximum_select_fusion.1), channel_id=1, source_target_pairs={{0,32},{8,40},{16,48},{24,56},{32,64},{40,72},{48,80},{56,88},{64,... | collective-permute-start | bytes 24584 | tf_op jit(solution)/shard_map/ppermute | solution.py:12
  56.7 18.2 %copy-start.29 = (f32[1,512]{1,0:T(1,128)}, f32[1,512]{1,0:T(1,128)S(1)}, u32[]{:S(2)}) copy-start(f32[1,512]{1,0:T(1,128)S(1)} %get-tuple-element.315) | copy-start | bytes 6148
  56.7 18.2 %copy-start.31 = (f32[1,512]{1,0:T(1,128)}, f32[1,512]{1,0:T(1,128)S(1)}, u32[]{:S(2)}) copy-start(f32[1,512]{1,0:T(1,128)S(1)} %get-tuple-element.316) | copy-start | bytes 6148
  56.7 18.2 %copy-start.33 = (f32[1,512]{1,0:T(1,128)}, f32[1,512]{1,0:T(1,128)S(1)}, u32[]{:S(2)}) copy-start(f32[1,512]{1,0:T(1,128)S(1)} %get-tuple-element.317) | copy-start | bytes 6148
  56.8 18.2 %copy-start.35 = (f32[1,512]{1,0:T(1,128)}, f32[1,512]{1,0:T(1,128)S(1)}, u32[]{:S(2)}) copy-start(f32[1,512]{1,0:T(1,128)S(1)} %get-tuple-element.318) | copy-start | bytes 6148
  56.8 10.5 %collective-permute-start.5 = (f32[4,512]{1,0:T(4,128)S(1)}, f32[4,512]{1,0:T(4,128)S(1)}, u32[]{:S(2)}, u32[]{:S(2)}) collective-permute-start(f32[4,512]{1,0:T(4,128)S(1)} %maximum_select_fusion.2), channel_id=1, source_target_pairs={{0,64},{8,72},{16,80},{24,88},{32,96},{40,104},{48,112},{56,120},{... | collective-permute-start | bytes 24584 | tf_op jit(solution)/shard_map/ppermute | solution.py:12
  67.3 7.7 %copy-start.41 = (f32[1,512]{1,0:T(1,128)}, f32[1,512]{1,0:T(1,128)S(1)}, u32[]{:S(2)}) copy-start(f32[1,512]{1,0:T(1,128)S(1)} %get-tuple-element.311) | copy-start | bytes 6148
  67.3 7.7 %copy-start.43 = (f32[1,512]{1,0:T(1,128)}, f32[1,512]{1,0:T(1,128)S(1)}, u32[]{:S(2)}) copy-start(f32[1,512]{1,0:T(1,128)S(1)} %get-tuple-element.312) | copy-start | bytes 6148
  67.3 7.7 %copy-start.45 = (f32[1,512]{1,0:T(1,128)}, f32[1,512]{1,0:T(1,128)S(1)}, u32[]{:S(2)}) copy-start(f32[1,512]{1,0:T(1,128)S(1)} %get-tuple-element.313) | copy-start | bytes 6148
  67.3 7.7 %copy-start.47 = (f32[1,512]{1,0:T(1,128)}, f32[1,512]{1,0:T(1,128)S(1)}, u32[]{:S(2)}) copy-start(f32[1,512]{1,0:T(1,128)S(1)} %get-tuple-element.314) | copy-start | bytes 6148
  67.4 7.4 %collective-permute-start.6 = (f32[4,512]{1,0:T(4,128)S(1)}, f32[4,512]{1,0:T(4,128)S(1)}, u32[]{:S(2)}, u32[]{:S(2)}) collective-permute-start(f32[4,512]{1,0:T(4,128)S(1)} %maximum_select_fusion.3), channel_id=1, source_target_pairs={{0,128},{8,136},{16,144},{24,152},{32,160},{40,168},{48,176},{56,1... | collective-permute-start | bytes 24584 | tf_op jit(solution)/shard_map/ppermute | solution.py:12
  76.1 36.8 %collective-permute-start.7 = (f32[4,512]{1,0:T(4,128)}, f32[4,512]{1,0:T(4,128)}, u32[]{:S(2)}, u32[]{:S(2)}) collective-permute-start(f32[4,512]{1,0:T(4,128)} %maximum_select_fusion.4), channel_id=1, source_target_pairs={{0,256},{8,264},{16,272},{24,280},{32,288},{40,296},{48,304},{56,3... | collective-permute-start | bytes 24584 | tf_op jit(solution)/shard_map/ppermute | solution.py:12
  111.7 2.2 copy-start.68
  112.6 2.3 copy-start.6
  112.6 2.3 copy-start.7
  112.7 2.3 copy-start.8
  132.1 1.7 copy-start.38
  132.1 2.7 copy-start.11
  132.1 2.7 copy-start.12
  137.2 5.5 %collective-permute-start.8 = (f32[4,512]{1,0:T(4,128)S(1)}, f32[4,512]{1,0:T(4,128)S(1)}, u32[]{:S(2)}, u32[]{:S(2)}) collective-permute-start(f32[4,512]{1,0:T(4,128)S(1)} %fusion.50), channel_id=1, source_target_pairs={{8,0},{16,8},{24,16},{32,24},{40,32},{48,40},{56,48},{64,56},{72,6... | collective-permute-start | bytes 24584 | tf_op jit(solution)/shard_map/ppermute | solution.py:12
  142.7 5.5 %collective-permute-start.9 = (f32[4,512]{1,0:T(4,128)S(1)}, f32[4,512]{1,0:T(4,128)S(1)}, u32[]{:S(2)}, u32[]{:S(2)}) collective-permute-start(f32[4,512]{1,0:T(4,128)S(1)} %broadcast_select_fusion.4), channel_id=1, source_target_pairs={{8,0},{16,8},{24,16},{32,24},{40,32},{48,40},{56,48},{64,56},{72,6... | collective-permute-start | bytes 24584 | tf_op jit(solution)/shard_map/ppermute | solution.py:12
  148.3 6.4 %collective-permute-start.10 = (f32[4,512]{1,0:T(4,128)S(1)}, f32[4,512]{1,0:T(4,128)S(1)}, u32[]{:S(2)}, u32[]{:S(2)}) collective-permute-start(f32[4,512]{1,0:T(4,128)S(1)} %maximum_select_fusion.6), channel_id=1, source_target_pairs={{16,0},{24,8},{32,16},{40,24},{48,32},{56,40},{64,48},{72,56},{80,... | collective-permute-start | bytes 24584 | tf_op jit(solution)/shard_map/ppermute | solution.py:12
  154.8 9.5 %collective-permute-start.11 = (f32[4,512]{1,0:T(4,128)S(1)}, f32[4,512]{1,0:T(4,128)S(1)}, u32[]{:S(2)}, u32[]{:S(2)}) collective-permute-start(f32[4,512]{1,0:T(4,128)S(1)} %maximum_select_fusion.7), channel_id=1, source_target_pairs={{32,0},{40,8},{48,16},{56,24},{64,32},{72,40},{80,48},{88,56},{96,... | collective-permute-start | bytes 24584 | tf_op jit(solution)/shard_map/ppermute | solution.py:12
  164.3 5.6 %collective-permute-start.12 = (f32[4,512]{1,0:T(4,128)S(1)}, f32[4,512]{1,0:T(4,128)S(1)}, u32[]{:S(2)}, u32[]{:S(2)}) collective-permute-start(f32[4,512]{1,0:T(4,128)S(1)} %maximum_select_fusion.8), channel_id=1, source_target_pairs={{64,0},{72,8},{80,16},{88,24},{96,32},{104,40},{112,48},{120,56},{... | collective-permute-start | bytes 24584 | tf_op jit(solution)/shard_map/ppermute | solution.py:12
  170.0 6.4 %collective-permute-start.13 = (f32[4,512]{1,0:T(4,128)S(1)}, f32[4,512]{1,0:T(4,128)S(1)}, u32[]{:S(2)}, u32[]{:S(2)}) collective-permute-start(f32[4,512]{1,0:T(4,128)S(1)} %maximum_select_fusion.9), channel_id=1, source_target_pairs={{128,0},{136,8},{144,16},{152,24},{160,32},{168,40},{176,48},{184,... | collective-permute-start | bytes 24584 | tf_op jit(solution)/shard_map/ppermute | solution.py:12
  176.5 9.5 %collective-permute-start.14 = (f32[4,512]{1,0:T(4,128)S(1)}, f32[4,512]{1,0:T(4,128)S(1)}, u32[]{:S(2)}, u32[]{:S(2)}) collective-permute-start(f32[4,512]{1,0:T(4,128)S(1)} %maximum_select_fusion.10), channel_id=1, source_target_pairs={{256,0},{264,8},{272,16},{280,24},{288,32},{296,40},{304,48},{312,... | collective-permute-start | bytes 24584 | tf_op jit(solution)/shard_map/ppermute | solution.py:12
  192.1 162.0 %all-reduce.8.cloned.1.call-start = ((), (), s32[]{:S(2)}) async-start(), calls=%async_computation.1 | async-start | bytes 1064960 | tf_op jit(solution)/shard_map/psum | solution.py:219
  272.7 8.3 %collective-permute-start.15 = (f32[3,512]{0,1:T(8,128)S(1)}, f32[3,512]{0,1:T(8,128)S(1)}, u32[]{:S(2)}, u32[]{:S(2)}) collective-permute-start(f32[3,512]{0,1:T(8,128)S(1)} %bitcast.248), channel_id=1, source_target_pairs={{8,0},{16,8},{24,16},{32,24},{40,32},{48,40},{56,48},{64,56},{72,6... | collective-permute-start | bytes 18440 | tf_op jit(solution)/shard_map/ppermute | solution.py:12
  354.1 3.0 copy-start.13
  (60 other events, 48.4 us)
Sparse Core Ops, SparseCore 0:
  192.2 80.4 all-reduce.5
  275.1 78.9 all-reduce.7
where the time goes:
time: 366 us; the launch traced here: 365 us
  waiting for transfers between devices  204 us (56%)
  starting transfers between devices  70.7 us (19%)
  local copies, waits for them, and re-layouts  39.3 us (11%)
  other arithmetic  21.6 us (6%)
  between operations  15.8 us (4%)
  blocking collectives  10.2 us (3%)
    psum x2, waiting for transfers between devices, per_device(): packed = lax.psum(lax.psum(packed, 'y'), 'z')  152 us
    ppermute x16, starting transfers between devices, from_behind(): return lax.ppermute(value, axis, pairs)  70.6 us
    ppermute x16, waiting for transfers between devices, from_behind(): return lax.ppermute(value, axis, pairs)  51.6 us
    unnamed x189, local copies, waits for them, and re-layouts  15.2 us
    psum x1, blocking collectives, per_device(): squares = lax.psum(squares, 'chan')  10.2 us
  transfers between devices with their start and end apart: 18, of which 16 were waited for; matrix products, arithmetic and copies ran while one was open for 8% of the time, Pallas kernels for 0%

commit v1 on v0

--- a/solution.py
+++ b/solution.py
@@ -2,6 +2,7 @@
 import jax.numpy as jnp
 from jax import lax
 from jax.sharding import Mesh, PartitionSpec as P
+from jax.lax import axis_size, ppermute
 
 SEQ = ("z", "y")
 
@@ -153,7 +154,20 @@
     squares = jnp.sum(mixed * mixed, axis=1)
     scaled = cotangent.astype(jnp.float32) * norm_gain
     dots = jnp.sum(scaled * mixed, axis=1)
-    squares = lax.psum(squares, "chan")
+
+    def chunk_number(work_x, peer_axis="chan"):
+        world = axis_size(peer_axis)
+        f_now, found_now = (work_x, 0)
+        while 1 << found_now < world:
+            by_rank = []
+            for h in range(world):
+                by_rank.append((h, h ^ 1 << found_now))
+            after = ppermute(f_now, peer_axis, by_rank)
+            f_now = f_now + after
+            found_now = found_now + 1
+        return f_now
+
+    squares = chunk_number(squares)
     model_width = local_width * lax.axis_size("chan")
     inverse = lax.rsqrt(squares / model_width + 1e-06)
     normed = (mixed * inverse[:, None] * norm_gain).astype(jnp.bfloat16)

time: 366 us -> 375 us (1.025)
  starting transfers between devices: 70.7 us -> 79.1 us
    ppermute x0 -> x3, starting transfers between devices: none -> 8.37 us  [chunk_number(): after = ppermute(f_now, peer_axis, by_rank)]
    unnamed x189 -> x179, local copies, waits for them, and re-layouts: 15.2 us -> 14 us
  transfers between devices with their start and end apart: 18 -> 21, of which waited for: 16 -> 18; matrix products, arithmetic and copies ran while one was open for 8% -> 8% of each run, Pallas kernels for 0% -> 0%
where the time goes in v1:
time: 375 us; the launch traced here: 374 us
  waiting for transfers between devices  207 us (55%)
  starting transfers between devices  79.1 us (21%)
  local copies, waits for them, and re-layouts  36.4 us (10%)
  other arithmetic  21.6 us (6%)
  between operations  15.8 us (4%)
  blocking collectives  10.6 us (3%)
    psum x2, waiting for transfers between devices, per_device(): packed = lax.psum(lax.psum(packed, 'y'), 'z')  152 us
    ppermute x16, starting transfers between devices, from_behind(): return lax.ppermute(value, axis, pairs)  70.6 us
    ppermute x16, waiting for transfers between devices, from_behind(): return lax.ppermute(value, axis, pairs)  51.6 us
    unnamed x179, local copies, waits for them, and re-layouts  14 us
    psum x1, blocking collectives, per_device(): dots = lax.psum(dots, 'chan')  10.6 us
    ppermute x3, starting transfers between devices, chunk_number(): after = ppermute(f_now, peer_axis, by_rank)  8.37 us
  transfers between devices with their start and end apart: 21, of which 18 were waited for; matrix products, arithmetic and copies ran while one was open for 8% of the time, Pallas kernels for 0%

profile of v1, /device:TPU:2, one launch (start us, length us, event | category | flops | bytes accessed | tf_op | source)
XLA Modules:
  0.0 374.0 jit_solution(6204604352598977779)
XLA Ops:
  8.2 3.5 collective-permute-start
  15.0 1.3 fusion.68
  16.3 2.5 multiply_cosine_fusion.1
  21.1 1.1 fusion.18
  27.3 3.5 collective-permute-start.1
  30.8 1.3 collective-permute-done.1
  32.2 4.2 %collective-permute-start.2 = (f32[4,512]{1,0:T(4,128)S(1)}, f32[4,512]{1,0:T(4,128)S(1)}, u32[]{:S(2)}, u32[]{:S(2)}) collective-permute-start(f32[4,512]{1,0:T(4,128)S(1)} %broadcast_select_fusion.5), channel_id=1, source_target_pairs={{0,8},{8,16},{16,24},{24,32},{32,40},{40,48},{48,56},{56,64},{64,7... | collective-permute-start | bytes 24584 | tf_op jit(solution)/shard_map/ppermute | solution.py:13
  36.4 1.3 collective-permute-done.2
  37.8 5.7 %collective-permute-start.3 = (f32[4,512]{1,0:T(4,128)S(1)}, f32[4,512]{1,0:T(4,128)S(1)}, u32[]{:S(2)}, u32[]{:S(2)}) collective-permute-start(f32[4,512]{1,0:T(4,128)S(1)} %maximum_select_fusion), channel_id=1, source_target_pairs={{0,16},{8,24},{16,32},{24,40},{32,48},{40,56},{48,64},{56,72},{64,... | collective-permute-start | bytes 24584 | tf_op jit(solution)/shard_map/ppermute | solution.py:13
  43.5 1.3 collective-permute-done.3
  44.9 10.6 %collective-permute-start.4 = (f32[4,512]{1,0:T(4,128)S(1)}, f32[4,512]{1,0:T(4,128)S(1)}, u32[]{:S(2)}, u32[]{:S(2)}) collective-permute-start(f32[4,512]{1,0:T(4,128)S(1)} %maximum_select_fusion.1), channel_id=1, source_target_pairs={{0,32},{8,40},{16,48},{24,56},{32,64},{40,72},{48,80},{56,88},{64,... | collective-permute-start | bytes 24584 | tf_op jit(solution)/shard_map/ppermute | solution.py:13
  55.5 1.3 collective-permute-done.4
  56.9 9.1 %collective-permute-start.5 = (f32[4,512]{1,0:T(4,128)S(1)}, f32[4,512]{1,0:T(4,128)S(1)}, u32[]{:S(2)}, u32[]{:S(2)}) collective-permute-start(f32[4,512]{1,0:T(4,128)S(1)} %maximum_select_fusion.2), channel_id=1, source_target_pairs={{0,64},{8,72},{16,80},{24,88},{32,96},{40,104},{48,112},{56,120},{... | collective-permute-start | bytes 24584 | tf_op jit(solution)/shard_map/ppermute | solution.py:13
  66.0 1.3 collective-permute-done.5
  67.5 6.1 %collective-permute-start.6 = (f32[4,512]{1,0:T(4,128)S(1)}, f32[4,512]{1,0:T(4,128)S(1)}, u32[]{:S(2)}, u32[]{:S(2)}) collective-permute-start(f32[4,512]{1,0:T(4,128)S(1)} %maximum_select_fusion.3), channel_id=1, source_target_pairs={{0,128},{8,136},{16,144},{24,152},{32,160},{40,168},{48,176},{56,1... | collective-permute-start | bytes 24584 | tf_op jit(solution)/shard_map/ppermute | solution.py:13
  73.6 1.3 collective-permute-done.6
  76.2 17.7 %collective-permute-start.7 = (f32[4,512]{1,0:T(4,128)}, f32[4,512]{1,0:T(4,128)}, u32[]{:S(2)}, u32[]{:S(2)}) collective-permute-start(f32[4,512]{1,0:T(4,128)} %maximum_select_fusion.4), channel_id=1, source_target_pairs={{0,256},{8,264},{16,272},{24,280},{32,288},{40,296},{48,304},{56,3... | collective-permute-start | bytes 24584 | tf_op jit(solution)/shard_map/ppermute | solution.py:13
  96.8 1.1 sub.357
  101.9 1.0 copy.140
  107.1 1.1 squeeze.79
  113.7 2.7 subtract_convert_fusion
  117.9 1.9 collective-permute-start.8
  119.8 1.1 collective-permute-done.8
  120.9 2.4 collective-permute-start.9
  124.2 2.2 collective-permute-done.9
  126.4 4.0 %collective-permute-start.10 = (f32[128]{0:T(128)S(1)}, f32[128]{0:T(128)S(1)}, u32[]{:S(2)}, u32[]{:S(2)}) collective-permute-start(f32[128]{0:T(128)S(1)} %add.435), channel_id=1, source_target_pairs={{0,4},{1,5},{2,6},{3,7},{4,0},{5,1},{6,2},{7,3},{8,12},{9,13},{10,... | collective-permute-start | bytes 1544 | tf_op jit(solution)/shard_map/ppermute | solution.py:165
  130.4 10.6 %psum.35 = f32[128]{0:T(128)S(1)} all-reduce(f32[128]{0:T(128)S(1)} %get-tuple-element.184), channel_id=1, replica_groups=mesh['z'=8,'y'=8,'chan'=8] {'chan'}, use_global_device_ids=true, to_apply=%region_8.9 | all-reduce | flops 128 | bytes 1024 | tf_op jit(solution)/shard_map/psum | solution.py:174
  146.3 1.3 collective-permute-start.11
  147.6 4.2 %collective-permute-done.11 = f32[4,512]{1,0:T(4,128)S(1)} collective-permute-done((f32[4,512]{1,0:T(4,128)S(1)}, f32[4,512]{1,0:T(4,128)S(1)}, u32[]{:S(2)}, u32[]{:S(2)}) %collective-permute-start.11) | collective-permute-done | bytes 8224 | tf_op jit(solution)/shard_map/ppermute | solution.py:13
  151.9 1.3 collective-permute-start.12
  153.2 4.2 %collective-permute-done.12 = f32[4,512]{1,0:T(4,128)S(1)} collective-permute-done((f32[4,512]{1,0:T(4,128)S(1)}, f32[4,512]{1,0:T(4,128)S(1)}, u32[]{:S(2)}, u32[]{:S(2)}) %collective-permute-start.12) | collective-permute-done | bytes 8224 | tf_op jit(solution)/shard_map/ppermute | solution.py:13
  157.5 1.3 collective-permute-start.13
  158.8 5.1 %collective-permute-done.13 = f32[4,512]{1,0:T(4,128)S(1)} collective-permute-done((f32[4,512]{1,0:T(4,128)S(1)}, f32[4,512]{1,0:T(4,128)S(1)}, u32[]{:S(2)}, u32[]{:S(2)}) %collective-permute-start.13) | collective-permute-done | bytes 8224 | tf_op jit(solution)/shard_map/ppermute | solution.py:13
  164.0 1.3 collective-permute-start.14
  165.3 8.1 %collective-permute-done.14 = f32[4,512]{1,0:T(4,128)S(1)} collective-permute-done((f32[4,512]{1,0:T(4,128)S(1)}, f32[4,512]{1,0:T(4,128)S(1)}, u32[]{:S(2)}, u32[]{:S(2)}) %collective-permute-start.14) | collective-permute-done | bytes 8224 | tf_op jit(solution)/shard_map/ppermute | solution.py:13
  173.5 1.3 collective-permute-start.15
  174.8 4.3 %collective-permute-done.15 = f32[4,512]{1,0:T(4,128)S(1)} collective-permute-done((f32[4,512]{1,0:T(4,128)S(1)}, f32[4,512]{1,0:T(4,128)S(1)}, u32[]{:S(2)}, u32[]{:S(2)}) %collective-permute-start.15) | collective-permute-done | bytes 8224 | tf_op jit(solution)/shard_map/ppermute | solution.py:13
  179.1 1.3 collective-permute-start.16
  181.4 4.1 %collective-permute-done.16 = f32[4,512]{1,0:T(4,128)S(1)} collective-permute-done((f32[4,512]{1,0:T(4,128)S(1)}, f32[4,512]{1,0:T(4,128)S(1)}, u32[]{:S(2)}, u32[]{:S(2)}) %collective-permute-start.16) | collective-permute-done | bytes 8224 | tf_op jit(solution)/shard_map/ppermute | solution.py:13
  185.6 1.3 collective-permute-start.17
  186.9 1.0 fusion.35
  187.9 7.2 %collective-permute-done.17 = f32[4,512]{1,0:T(4,128)S(1)} collective-permute-done((f32[4,512]{1,0:T(4,128)S(1)}, f32[4,512]{1,0:T(4,128)S(1)}, u32[]{:S(2)}, u32[]{:S(2)}) %collective-permute-start.17) | collective-permute-done | bytes 8224 | tf_op jit(solution)/shard_map/ppermute | solution.py:13
  195.9 1.1 multiply_subtract_fusion
  201.3 80.8 %all-reduce.5.cloned.1.call-done = (f32[67584]{0:T(1024)}, f32[8,64,128]{2,1,0:T(8,128)}) async-done(((f32[67584]{0:T(1024)}, f32[8,64,128]{2,1,0:T(8,128)}), (f32[67584]{0:T(1024)}, f32[8,64,128]{2,1,0:T(8,128)})) %all-reduce.5.cloned.1.call-update) | async-done | bytes 532496 | tf_op jit(solution)/shard_map/psum | solution.py:233
  282.1 1.3 collective-permute-start.18
  284.2 6.2 %collective-permute-done.18 = f32[3,512]{0,1:T(8,128)S(1)} collective-permute-done((f32[3,512]{0,1:T(8,128)S(1)}, f32[3,512]{0,1:T(8,128)S(1)}, u32[]{:S(2)}, u32[]{:S(2)}) %collective-permute-start.18) | collective-permute-done | bytes 6176 | tf_op jit(solution)/shard_map/ppermute | solution.py:13
  291.9 71.5 %all-reduce.7.cloned.1.call-done = (f32[67584]{0:T(1024)}, f32[8,64,128]{2,1,0:T(8,128)}) async-done(((f32[67584]{0:T(1024)}, f32[8,64,128]{2,1,0:T(8,128)}), (f32[67584]{0:T(1024)}, f32[8,64,128]{2,1,0:T(8,128)})) %all-reduce.7.cloned.1.call-update) | async-done | bytes 532496 | tf_op jit(solution)/shard_map/psum | solution.py:233
  363.4 1.7 slice.228
  (357 shorter events, 47.4 us)
Async XLA Ops:
  7.2 109.3 %copy-start = (bf16[8,64,128]{2,1,0:T(8,128)(2,1)S(1)}, bf16[8,64,128]{2,1,0:T(8,128)(2,1)}, u32[]{:S(2)}) copy-start(bf16[8,64,128]{2,1,0:T(8,128)(2,1)} %param.19) | copy-start | bytes 393220
  7.2 274.9 %all-reduce.5.cloned.1.call-start = ((), (), s32[]{:S(2)}) async-start(), calls=%async_computation | async-start | bytes 1064960 | tf_op jit(solution)/shard_map/psum | solution.py:233
  8.1 3.5 copy-start.84
  8.2 14.0 %collective-permute-start = (bf16[3,512]{0,1:T(8,128)(2,1)S(1)}, bf16[3,512]{0,1:T(8,128)(2,1)S(1)}, u32[]{:S(2)}, u32[]{:S(2)}) collective-permute-start(bf16[3,512]{0,1:T(8,128)(2,1)S(1)} %copy.131), channel_id=1, source_target_pairs={{0,8},{8,16},{16,24},{24,32},{32,40},{40,48},{48,56},{56,64},{64,7... | collective-permute-start | bytes 9224 | tf_op jit(solution)/shard_map/ppermute | solution.py:13
  14.3 4.5 %copy-start.70 = (f32[2,64]{1,0:T(2,128)}, f32[2,64]{1,0:T(2,128)S(1)}, u32[]{:S(2)}) copy-start(f32[2,64]{1,0:T(2,128)S(1)} %reduce.6) | copy-start | bytes 1540
  16.3 8.4 %copy-start.55 = (f32[512]{0:T(512)}, f32[512]{0:T(512)S(1)}, u32[]{:S(2)}) copy-start(f32[512]{0:T(512)S(1)} %get-tuple-element.356) | copy-start | bytes 6148
  16.3 11.0 %copy-start.57 = (f32[512]{0:T(512)}, f32[512]{0:T(512)S(1)}, u32[]{:S(2)}) copy-start(f32[512]{0:T(512)S(1)} %get-tuple-element.352) | copy-start | bytes 6148
  20.3 2.0 copy-start.47
  20.3 2.0 copy-start.49
  20.4 2.0 copy-start.51
  20.4 2.0 copy-start.53
  27.3 4.8 %collective-permute-start.1 = (f32[4,512]{1,0:T(4,128)S(1)}, f32[4,512]{1,0:T(4,128)S(1)}, u32[]{:S(2)}, u32[]{:S(2)}) collective-permute-start(f32[4,512]{1,0:T(4,128)S(1)} %fusion.48), channel_id=1, source_target_pairs={{0,8},{8,16},{16,24},{24,32},{32,40},{40,48},{48,56},{56,64},{64,7... | collective-permute-start | bytes 24584 | tf_op jit(solution)/shard_map/ppermute | solution.py:13
  32.2 5.5 %collective-permute-start.2 = (f32[4,512]{1,0:T(4,128)S(1)}, f32[4,512]{1,0:T(4,128)S(1)}, u32[]{:S(2)}, u32[]{:S(2)}) collective-permute-start(f32[4,512]{1,0:T(4,128)S(1)} %broadcast_select_fusion.5), channel_id=1, source_target_pairs={{0,8},{8,16},{16,24},{24,32},{32,40},{40,48},{48,56},{56,64},{64,7... | collective-permute-start | bytes 24584 | tf_op jit(solution)/shard_map/ppermute | solution.py:13
  37.8 7.1 %collective-permute-start.3 = (f32[4,512]{1,0:T(4,128)S(1)}, f32[4,512]{1,0:T(4,128)S(1)}, u32[]{:S(2)}, u32[]{:S(2)}) collective-permute-start(f32[4,512]{1,0:T(4,128)S(1)} %maximum_select_fusion), channel_id=1, source_target_pairs={{0,16},{8,24},{16,32},{24,40},{32,48},{40,56},{48,64},{56,72},{64,... | collective-permute-start | bytes 24584 | tf_op jit(solution)/shard_map/ppermute | solution.py:13
  44.8 30.2 %copy-start.17 = (f32[1,512]{1,0:T(1,128)}, f32[1,512]{1,0:T(1,128)S(1)}, u32[]{:S(2)}) copy-start(f32[1,512]{1,0:T(1,128)S(1)} %get-tuple-element.319) | copy-start | bytes 6148
  44.8 30.2 %copy-start.19 = (f32[1,512]{1,0:T(1,128)}, f32[1,512]{1,0:T(1,128)S(1)}, u32[]{:S(2)}) copy-start(f32[1,512]{1,0:T(1,128)S(1)} %get-tuple-element.320) | copy-start | bytes 6148
  44.9 30.2 %copy-start.21 = (f32[1,512]{1,0:T(1,128)}, f32[1,512]{1,0:T(1,128)S(1)}, u32[]{:S(2)}) copy-start(f32[1,512]{1,0:T(1,128)S(1)} %get-tuple-element.321) | copy-start | bytes 6148
  44.9 30.2 %copy-start.23 = (f32[1,512]{1,0:T(1,128)}, f32[1,512]{1,0:T(1,128)S(1)}, u32[]{:S(2)}) copy-start(f32[1,512]{1,0:T(1,128)S(1)} %get-tuple-element.322) | copy-start | bytes 6148
  44.9 11.9 %collective-permute-start.4 = (f32[4,512]{1,0:T(4,128)S(1)}, f32[4,512]{1,0:T(4,128)S(1)}, u32[]{:S(2)}, u32[]{:S(2)}) collective-permute-start(f32[4,512]{1,0:T(4,128)S(1)} %maximum_select_fusion.1), channel_id=1, source_target_pairs={{0,32},{8,40},{16,48},{24,56},{32,64},{40,72},{48,80},{56,88},{64,... | collective-permute-start | bytes 24584 | tf_op jit(solution)/shard_map/ppermute | solution.py:13
  56.8 18.2 %copy-start.27 = (f32[1,512]{1,0:T(1,128)}, f32[1,512]{1,0:T(1,128)S(1)}, u32[]{:S(2)}) copy-start(f32[1,512]{1,0:T(1,128)S(1)} %get-tuple-element.315) | copy-start | bytes 6148
  56.8 18.2 %copy-start.29 = (f32[1,512]{1,0:T(1,128)}, f32[1,512]{1,0:T(1,128)S(1)}, u32[]{:S(2)}) copy-start(f32[1,512]{1,0:T(1,128)S(1)} %get-tuple-element.316) | copy-start | bytes 6148
  56.9 18.2 %copy-start.31 = (f32[1,512]{1,0:T(1,128)}, f32[1,512]{1,0:T(1,128)S(1)}, u32[]{:S(2)}) copy-start(f32[1,512]{1,0:T(1,128)S(1)} %get-tuple-element.317) | copy-start | bytes 6148
  56.9 18.2 %copy-start.33 = (f32[1,512]{1,0:T(1,128)}, f32[1,512]{1,0:T(1,128)S(1)}, u32[]{:S(2)}) copy-start(f32[1,512]{1,0:T(1,128)S(1)} %get-tuple-element.318) | copy-start | bytes 6148
  56.9 10.5 %collective-permute-start.5 = (f32[4,512]{1,0:T(4,128)S(1)}, f32[4,512]{1,0:T(4,128)S(1)}, u32[]{:S(2)}, u32[]{:S(2)}) collective-permute-start(f32[4,512]{1,0:T(4,128)S(1)} %maximum_select_fusion.2), channel_id=1, source_target_pairs={{0,64},{8,72},{16,80},{24,88},{32,96},{40,104},{48,112},{56,120},{... | collective-permute-start | bytes 24584 | tf_op jit(solution)/shard_map/ppermute | solution.py:13
  67.4 7.7 %copy-start.39 = (f32[1,512]{1,0:T(1,128)}, f32[1,512]{1,0:T(1,128)S(1)}, u32[]{:S(2)}) copy-start(f32[1,512]{1,0:T(1,128)S(1)} %get-tuple-element.311) | copy-start | bytes 6148
  67.4 7.7 %copy-start.41 = (f32[1,512]{1,0:T(1,128)}, f32[1,512]{1,0:T(1,128)S(1)}, u32[]{:S(2)}) copy-start(f32[1,512]{1,0:T(1,128)S(1)} %get-tuple-element.312) | copy-start | bytes 6148
  67.4 7.7 %copy-start.43 = (f32[1,512]{1,0:T(1,128)}, f32[1,512]{1,0:T(1,128)S(1)}, u32[]{:S(2)}) copy-start(f32[1,512]{1,0:T(1,128)S(1)} %get-tuple-element.313) | copy-start | bytes 6148
  67.4 7.7 %copy-start.45 = (f32[1,512]{1,0:T(1,128)}, f32[1,512]{1,0:T(1,128)S(1)}, u32[]{:S(2)}) copy-start(f32[1,512]{1,0:T(1,128)S(1)} %get-tuple-element.314) | copy-start | bytes 6148
  67.5 7.4 %collective-permute-start.6 = (f32[4,512]{1,0:T(4,128)S(1)}, f32[4,512]{1,0:T(4,128)S(1)}, u32[]{:S(2)}, u32[]{:S(2)}) collective-permute-start(f32[4,512]{1,0:T(4,128)S(1)} %maximum_select_fusion.3), channel_id=1, source_target_pairs={{0,128},{8,136},{16,144},{24,152},{32,160},{40,168},{48,176},{56,1... | collective-permute-start | bytes 24584 | tf_op jit(solution)/shard_map/ppermute | solution.py:13
  76.2 34.9 %collective-permute-start.7 = (f32[4,512]{1,0:T(4,128)}, f32[4,512]{1,0:T(4,128)}, u32[]{:S(2)}, u32[]{:S(2)}) collective-permute-start(f32[4,512]{1,0:T(4,128)} %maximum_select_fusion.4), channel_id=1, source_target_pairs={{0,256},{8,264},{16,272},{24,280},{32,288},{40,296},{48,304},{56,3... | collective-permute-start | bytes 24584 | tf_op jit(solution)/shard_map/ppermute | solution.py:13
  110.0 2.2 copy-start.66
  110.9 2.2 copy-start.6
  110.9 2.2 copy-start.7
  110.9 2.2 copy-start.8
  117.9 3.1 collective-permute-start.8
  120.9 5.5 %collective-permute-start.9 = (f32[128]{0:T(128)S(1)}, f32[128]{0:T(128)S(1)}, u32[]{:S(2)}, u32[]{:S(2)}) collective-permute-start(f32[128]{0:T(128)S(1)} %add.434), channel_id=1, source_target_pairs={{0,2},{1,3},{2,0},{3,1},{4,6},{5,7},{6,4},{7,5},{8,10},{9,11},{10,... | collective-permute-start | bytes 1544 | tf_op jit(solution)/shard_map/ppermute | solution.py:165
  126.4 14.6 %collective-permute-start.10 = (f32[128]{0:T(128)S(1)}, f32[128]{0:T(128)S(1)}, u32[]{:S(2)}, u32[]{:S(2)}) collective-permute-start(f32[128]{0:T(128)S(1)} %add.435), channel_id=1, source_target_pairs={{0,4},{1,5},{2,6},{3,7},{4,0},{5,1},{6,2},{7,3},{8,12},{9,13},{10,... | collective-permute-start | bytes 1544 | tf_op jit(solution)/shard_map/ppermute | solution.py:165
  142.6 2.0 copy-start.11
  146.3 5.5 %collective-permute-start.11 = (f32[4,512]{1,0:T(4,128)S(1)}, f32[4,512]{1,0:T(4,128)S(1)}, u32[]{:S(2)}, u32[]{:S(2)}) collective-permute-start(f32[4,512]{1,0:T(4,128)S(1)} %fusion.50), channel_id=1, source_target_pairs={{8,0},{16,8},{24,16},{32,24},{40,32},{48,40},{56,48},{64,56},{72,6... | collective-permute-start | bytes 24584 | tf_op jit(solution)/shard_map/ppermute | solution.py:13
  151.9 5.5 %collective-permute-start.12 = (f32[4,512]{1,0:T(4,128)S(1)}, f32[4,512]{1,0:T(4,128)S(1)}, u32[]{:S(2)}, u32[]{:S(2)}) collective-permute-start(f32[4,512]{1,0:T(4,128)S(1)} %broadcast_select_fusion.4), channel_id=1, source_target_pairs={{8,0},{16,8},{24,16},{32,24},{40,32},{48,40},{56,48},{64,56},{72,6... | collective-permute-start | bytes 24584 | tf_op jit(solution)/shard_map/ppermute | solution.py:13
  157.5 6.4 %collective-permute-start.13 = (f32[4,512]{1,0:T(4,128)S(1)}, f32[4,512]{1,0:T(4,128)S(1)}, u32[]{:S(2)}, u32[]{:S(2)}) collective-permute-start(f32[4,512]{1,0:T(4,128)S(1)} %maximum_select_fusion.6), channel_id=1, source_target_pairs={{16,0},{24,8},{32,16},{40,24},{48,32},{56,40},{64,48},{72,56},{80,... | collective-permute-start | bytes 24584 | tf_op jit(solution)/shard_map/ppermute | solution.py:13
  164.0 9.5 %collective-permute-start.14 = (f32[4,512]{1,0:T(4,128)S(1)}, f32[4,512]{1,0:T(4,128)S(1)}, u32[]{:S(2)}, u32[]{:S(2)}) collective-permute-start(f32[4,512]{1,0:T(4,128)S(1)} %maximum_select_fusion.7), channel_id=1, source_target_pairs={{32,0},{40,8},{48,16},{56,24},{64,32},{72,40},{80,48},{88,56},{96,... | collective-permute-start | bytes 24584 | tf_op jit(solution)/shard_map/ppermute | solution.py:13
  173.5 5.6 %collective-permute-start.15 = (f32[4,512]{1,0:T(4,128)S(1)}, f32[4,512]{1,0:T(4,128)S(1)}, u32[]{:S(2)}, u32[]{:S(2)}) collective-permute-start(f32[4,512]{1,0:T(4,128)S(1)} %maximum_select_fusion.8), channel_id=1, source_target_pairs={{64,0},{72,8},{80,16},{88,24},{96,32},{104,40},{112,48},{120,56},{... | collective-permute-start | bytes 24584 | tf_op jit(solution)/shard_map/ppermute | solution.py:13
  179.1 6.4 %collective-permute-start.16 = (f32[4,512]{1,0:T(4,128)S(1)}, f32[4,512]{1,0:T(4,128)S(1)}, u32[]{:S(2)}, u32[]{:S(2)}) collective-permute-start(f32[4,512]{1,0:T(4,128)S(1)} %maximum_select_fusion.9), channel_id=1, source_target_pairs={{128,0},{136,8},{144,16},{152,24},{160,32},{168,40},{176,48},{184,... | collective-permute-start | bytes 24584 | tf_op jit(solution)/shard_map/ppermute | solution.py:13
  185.6 9.5 %collective-permute-start.17 = (f32[4,512]{1,0:T(4,128)S(1)}, f32[4,512]{1,0:T(4,128)S(1)}, u32[]{:S(2)}, u32[]{:S(2)}) collective-permute-start(f32[4,512]{1,0:T(4,128)S(1)} %maximum_select_fusion.10), channel_id=1, source_target_pairs={{256,0},{264,8},{272,16},{280,24},{288,32},{296,40},{304,48},{312,... | collective-permute-start | bytes 24584 | tf_op jit(solution)/shard_map/ppermute | solution.py:13
  201.2 162.2 %all-reduce.7.cloned.1.call-start = ((), (), s32[]{:S(2)}) async-start(), calls=%async_computation.1 | async-start | bytes 1064960 | tf_op jit(solution)/shard_map/psum | solution.py:233
  282.1 8.3 %collective-permute-start.18 = (f32[3,512]{0,1:T(8,128)S(1)}, f32[3,512]{0,1:T(8,128)S(1)}, u32[]{:S(2)}, u32[]{:S(2)}) collective-permute-start(f32[3,512]{0,1:T(8,128)S(1)} %bitcast.248), channel_id=1, source_target_pairs={{8,0},{16,8},{24,16},{32,24},{40,32},{48,40},{56,48},{64,56},{72,6... | collective-permute-start | bytes 18440 | tf_op jit(solution)/shard_map/ppermute | solution.py:13
  363.4 3.0 copy-start.13
  (58 other events, 49.2 us)
Sparse Core Ops, SparseCore 0:
  201.4 80.6 all-reduce.4
  284.5 78.8 all-reduce.6
